TPU v7x, 128 devices: a whole 4x4x4 slice. The times are simulated.
128 devices in a mesh: req: 4 (over z), vocab: 32 (over y, x, core).
Axes of the slice: x: 4, y: 4, z: 4, core: 2. Of those that a mesh axis runs over, the one named last changes fastest.
Arguments:
- hidden: bfloat16 [16, 1536, 2048], P('req', 'vocab'), may hold values from -80 to 80
- norm_gain: float32 [2048], replicated, may hold values from 0.6 to 1.4
- head_weight: bfloat16 [2048, 32000], P(None, 'vocab'), may hold values from -2 to 2
- token_ids: int32 [16, 1536], P('req', 'vocab'), may hold values from 0 to 31999
- lengths: int32 [16], replicated, may hold values from 1 to 1536, 15360 in all
- group_ids: int32 [16], replicated, may hold values from 0 to 3
Outputs:
- logprob: float32 [16, 1536], P('req', 'vocab')
- entropy: float32 [16, 1536], P('req', 'vocab')
- centered: float32 [16], replicated
Inputs may be any that keep to these rules, and one draw needn't show every extreme that they name: The lengths sum to 15360; the longest is 1536.
All inputs are finite; a program needn't handle non-finite values.
Results may differ from a plain program's by a relative error of at most 0.00093.
Values may be sent and summed in bfloat16 or wider, within the bound.
No kernel may reach another device: no remote copies, remote signals or barrier semaphores. Data moves between devices by JAX's collectives and lax.ppermute only.
A program may use at most 128 MiB of HBM per device.

v0:
```python
import jax
import jax.numpy as jnp
from jax import lax
from jax.sharding import PartitionSpec as P

norm_eps = 1e-06


def slice_stats(rows, tokens, weight, offset):
    row_count = rows.shape[0]
    block_len = min(512, row_count)
    columns = jnp.arange(weight.shape[1], dtype=jnp.int32)
    results = []
    for block_start in range(0, row_count, block_len):
        block_rows = rows[block_start : block_start + block_len]
        local_ids = tokens[block_start : block_start + block_len] - offset
        logits = jnp.dot(block_rows, weight, preferred_element_type=jnp.float32)
        row_top = jnp.max(logits, axis=1)
        exps = jnp.exp(logits - row_top[:, None])
        exp_total = jnp.sum(exps, axis=1)
        moment = jnp.sum(exps * logits, axis=1)
        picked = jnp.sum(jnp.where(columns[None, :] == local_ids[:, None], logits, 0.0), axis=1)
        results.append((row_top, exp_total, moment, picked))
    return tuple((jnp.concatenate([item[slot] for item in results]) for slot in range(4)))


def body(hidden, norm_gain, head_weight, token_ids, lengths, group_ids):
    req_dev, pos_dev, model_width = hidden.shape
    vocab_dev = head_weight.shape[1]
    vocab_index = lax.axis_index("vocab")
    req_index = lax.axis_index("req")
    values = hidden.astype(jnp.float32)
    squares = jnp.mean(values * values, axis=-1, keepdims=True)
    normed = (values * lax.rsqrt(squares + norm_eps) * norm_gain).astype(jnp.bfloat16)
    own_rows = req_dev * pos_dev
    flat_rows = normed.reshape(own_rows, model_width)
    flat_tokens = token_ids.reshape(own_rows)
    offset = vocab_index * vocab_dev
    fresh = slice_stats(
        lax.all_gather(flat_rows, "vocab", axis=0, tiled=True),
        lax.all_gather(flat_tokens, "vocab", axis=0, tiled=True),
        head_weight,
        offset,
    )
    maxima, sums, moments, picked = tuple((new_part for new_part in fresh))
    own_start = vocab_index * own_rows
    row_top = lax.pmax(maxima, "vocab")
    rescale = jnp.exp(maxima - row_top)
    exp_total, moment, token_logit = lax.psum((sums * rescale, moments * rescale, picked), "vocab")
    row_top = lax.dynamic_slice_in_dim(row_top, own_start, own_rows)
    exp_total = lax.dynamic_slice_in_dim(exp_total, own_start, own_rows)
    moment = lax.dynamic_slice_in_dim(moment, own_start, own_rows)
    token_logit = lax.dynamic_slice_in_dim(token_logit, own_start, own_rows)
    log_total = row_top + jnp.log(exp_total)
    raw_logprob = (token_logit - log_total).reshape(req_dev, pos_dev)
    raw_entropy = (log_total - moment / exp_total).reshape(req_dev, pos_dev)
    positions = vocab_index * pos_dev + jnp.arange(pos_dev, dtype=jnp.int32)
    own_lengths = lax.dynamic_slice_in_dim(lengths, req_index * req_dev, req_dev)
    is_live = positions[None, :] < own_lengths[:, None]
    logprob = jnp.where(is_live, raw_logprob, 0.0)
    entropy = jnp.where(is_live, raw_entropy, 0.0)
    partial_sums = jnp.sum(logprob, axis=1)
    request_count = lengths.shape[0]
    global_rows = req_index * req_dev + jnp.arange(req_dev, dtype=jnp.int32)
    slots = jnp.arange(request_count, dtype=jnp.int32)
    placed = jnp.sum(
        jnp.where(slots[None, :] == global_rows[:, None], partial_sums[:, None], 0.0), axis=0
    )
    seq_sum = lax.psum(placed, ("req", "vocab"))
    same = (group_ids[:, None] == group_ids[None, :]).astype(jnp.float32)
    members = jnp.sum(same, axis=1)
    group_mean = jnp.sum(same * seq_sum[None, :], axis=1) / members
    spread = jnp.sum(same * (seq_sum[None, :] - group_mean[:, None]) ** 2, axis=1) / members
    group_std = jnp.maximum(jnp.sqrt(spread), 1.0)
    centered = (seq_sum - group_mean) / group_std
    return (logprob, entropy, centered)


def solution(mesh):
    return jax.shard_map(
        body,
        mesh=mesh,
        in_specs=(P("req", "vocab", None), P(), P(None, "vocab"), P("req", "vocab"), P(), P()),
        out_specs=(P("req", "vocab"), P("req", "vocab"), P()),
        check_vma=False,
    )
```

profile of v0, /device:TPU:1, one launch (start us, length us, event | category | flops | bytes accessed | tf_op | source)
XLA Modules:
  0.0 505.1 jit_solution(15608291727772157882)
XLA Ops:
  7.2 0.0 copy-start.15
  7.2 0.0 copy-start.11
  7.2 0.0 all-gather.2.cloned.1.call-start
  7.2 1.4 fusion.36
  8.6 2.3 fusion.38
  10.9 0.0 all-gather.2.cloned.1.call-update
  11.0 0.0 all-reduce.4.cloned.1.call-start
  11.1 0.0 copy-done.11
  11.1 0.1 reshape.73
  11.2 0.0 copy-done.15
  11.2 0.6 dynamic-slice
  12.4 0.3 dynamic-update-slice
  12.7 127.5 %all-reduce = s32[6144]{0:T(1024)S(1)} all-reduce(s32[6144]{0:T(1024)S(1)} %dynamic-update-slice), channel_id=1, replica_groups=mesh['req'=4,'vocab'=32] {'vocab'}, use_global_device_ids=true, to_apply=%add | all-reduce | flops 6144 | bytes 49152
  140.2 0.0 all-gather.2.cloned.1.call-done
  140.2 0.0 copy-start.12
  140.2 6.6 %fusion.45 = (f32[512]{0:T(512)S(1)}, f32[512,1000]{0,1:T(8,128)}) fusion(bf16[2048,1000]{0,1:T(8,128)(2,1)} %param.8, bf16[6144,2048]{1,0:T(8,128)(2,1)} %all-gather.2.cloned.1.call-done), kind=kOutput, calls=%fused_computation.170 | convolution fusion | flops 2097663488 | bytes 8243200 | tf_op jit(solution)/shard_map/dot_general | solution.py:17
  146.9 4.1 copy-done.12
  150.9 5.9 %fusion.46 = (f32[512]{0:T(512)S(1)}, f32[512,1000]{0,1:T(8,128)}) fusion(bf16[2048,1000]{0,1:T(8,128)(2,1)} %param.8, bf16[6144,2048]{1,0:T(8,128)(2,1)S(1)} %copy-done.12), kind=kOutput, calls=%fused_computation.171 | convolution fusion | flops 2097663488 | bytes 8243200 | tf_op jit(solution)/shard_map/dot_general | solution.py:17
  156.9 0.0 copy-done.13
  156.9 3.6 fusion.47
  160.5 3.6 fusion.48
  164.1 3.7 fusion.49
  167.8 3.6 fusion.50
  171.5 3.8 fusion.51
  175.3 3.6 fusion.52
  178.9 3.6 fusion.53
  182.6 3.6 fusion.54
  186.2 2.3 fusion.55
  188.5 3.6 fusion.56
  192.1 124.0 %pmax.7 = f32[6144]{0:T(1024)S(1)} all-reduce(f32[6144]{0:T(1024)S(1)} %constant_dynamic-update-slice_fusion.1), channel_id=1, replica_groups=mesh['req'=4,'vocab'=32] {'vocab'}, use_global_device_ids=true, to_apply=%region_26.27 | all-reduce | flops 6144 | bytes 49152 | tf_op jit(solution)/shard_map/pmax | solution.py:47
  316.1 3.7 multiply_reduce_fusion.10
  319.8 0.0 copy-done.7
  319.8 0.0 copy-done.8
  319.8 0.0 copy-start.5
  319.8 0.0 copy-start.6
  319.8 1.3 multiply_reduce_fusion.8
  321.2 0.2 copy-done.5
  321.4 0.6 copy-done.6
  322.0 1.3 multiply_reduce_fusion.6
  323.4 0.2 copy-done.3
  323.6 0.6 copy-done.4
  324.2 1.3 multiply_reduce_fusion.4
  325.6 0.2 copy-done.1
  325.8 0.6 copy-done.2
  326.4 1.3 multiply_reduce_fusion.2
  327.8 0.2 copy-done
  328.0 1.3 multiply_reduce_fusion
  329.6 0.0 copy-start.9
  329.6 0.6 fusion.39
  330.3 0.0 copy-done.9
  330.3 0.0 all-reduce.4.cloned.1.call-update
  330.3 0.0 copy-done.14
  330.3 0.1 dynamic_slice.15
  330.4 100.8 %all-reduce.4.cloned.1.call-done = (f32[6144]{0:T(1024)}, f32[6144]{0:T(1024)}, f32[6144]{0:T(1024)}) async-done(((f32[6144]{0:T(1024)}, f32[6144]{0:T(1024)}, f32[6144]{0:T(1024)}), (f32[6144]{0:T(1024)}, f32[6144]{0:T(1024)}, f32[6144]{0:T(1024)})) %all-reduce.4.cloned.1.call-update) | async-done | bytes 73744 | tf_op jit(solution)/shard_map/psum | solution.py:49
  431.3 0.8 divide_subtract_fusion
  432.1 0.1 reshape.71
  432.2 0.1 reshape.72
  432.2 0.8 fusion.44
  433.0 0.1 select_reduce_fusion.12
  433.1 64.2 %psum.31 = f32[16]{0:T(128)S(1)} all-reduce(f32[16]{0:T(128)S(1)} %select_reduce_fusion.12), channel_id=1, replica_groups=mesh['req'=4,'vocab'=32] {'req','vocab'}, use_global_device_ids=true, to_apply=%region_55.56 | all-reduce | flops 16 | bytes 128 | tf_op jit(solution)/shard_map/psum | solution.py:69
  497.3 0.0 copy-done.10
  497.3 0.2 fusion.42
  497.5 0.2 fusion.43
  497.7 0.5 maximum_divide_fusion
  (68 shorter events, 0.3 us)
Async XLA Ops:
  7.2 4.0 copy-start.15
  7.2 3.9 copy-start.11
  7.2 133.0 %all-gather.2.cloned.1.call-start = ((), (), s32[]{:S(2)}) async-start(), calls=%async_computation | async-start | bytes 25952256 | tf_op jit(solution)/shard_map/all_gather | solution.py:40
  11.0 420.3 %all-reduce.4.cloned.1.call-start = ((), (), s32[]{:S(2)}) async-start(), calls=%async_computation.1 | async-start | bytes 147456 | tf_op jit(solution)/shard_map/psum | solution.py:49
  140.2 10.7 %copy-start.12 = (bf16[6144,2048]{1,0:T(8,128)(2,1)S(1)}, bf16[6144,2048]{1,0:T(8,128)(2,1)}, u32[]{:S(2)}) copy-start(bf16[6144,2048]{1,0:T(8,128)(2,1)} %all-gather.2.cloned.1.call-done) | copy-start | bytes 75497472
  150.9 5.9 %copy-start.13 = (bf16[2048,1000]{0,1:T(8,128)(2,1)S(1)}, bf16[2048,1000]{0,1:T(8,128)(2,1)}, u32[]{:S(2)}) copy-start(bf16[2048,1000]{0,1:T(8,128)(2,1)} %param.8) | copy-start | bytes 12288004
  316.1 3.7 copy-start.7
  316.1 3.7 copy-start.8
  319.8 1.6 copy-start.5
  319.8 2.2 copy-start.6
  322.0 1.6 copy-start.3
  322.0 2.2 copy-start.4
  324.2 1.6 copy-start.1
  324.2 2.2 copy-start.2
  326.4 1.6 copy-start
  328.0 2.4 copy-start.14
  328.0 169.3 %copy-start.10 = (s32[16]{0:T(128)S(1)}, s32[16]{0:T(128)}, u32[]{:S(2)}) copy-start(s32[16]{0:T(128)} %param.11) | copy-start | bytes 196
  329.6 0.6 copy-start.9
Sparse Core Ops, SparseCore 0:
  11.1 95.8 all-gather.1
  330.4 100.7 all-reduce.3
where the time goes:
time: 505 us
  blocking collectives  316 us (63%)
  waiting for transfers between devices  101 us (20%)
  matrix products  47.7 us (9%)
  other arithmetic  17.3 us (3%)
  between operations  15.1 us (3%)
  local copies, waits for them, and re-layouts  8.28 us (2%)
    unnamed x1, blocking collectives  127 us
    pmax x1, blocking collectives, body(): row_top = lax.pmax(maxima, 'vocab')  124 us
    psum x1, waiting for transfers between devices, body(): lax.psum((sums * rescale, moments * rescale, picked), 'vocab')  101 us
    psum x1, blocking collectives, body(): seq_sum = lax.psum(placed, ('req', 'vocab'))  64.2 us
    dot_general x12, matrix products, slice_stats(): logits = jnp.dot(block_rows, weight, preferred_element_type=jnp.float32)  47.7 us
    reduce_sum x6, other arithmetic, slice_stats(): moment = jnp.sum(exps * logits, axis=1)  10.3 us
  transfers between devices with their start and end apart: 2, of which 1 were waited for; matrix products, arithmetic and copies ran while one was open for 0% of the time, Pallas kernels for 0%

commit v1 on v0

--- a/solution.py
+++ b/solution.py
@@ -4,6 +4,11 @@
 from jax.sharding import PartitionSpec as P
 
 norm_eps = 1e-06
+
+
+def gather_and_add(x, name):
+    pieces = lax.all_gather(x, name)
+    return jnp.sum(pieces, axis=0)
 
 
 def slice_stats(rows, tokens, weight, offset):
@@ -66,7 +71,7 @@
     placed = jnp.sum(
         jnp.where(slots[None, :] == global_rows[:, None], partial_sums[:, None], 0.0), axis=0
     )
-    seq_sum = lax.psum(placed, ("req", "vocab"))
+    seq_sum = gather_and_add(placed, ("req", "vocab"))
     same = (group_ids[:, None] == group_ids[None, :]).astype(jnp.float32)
     members = jnp.sum(same, axis=1)
     group_mean = jnp.sum(same * seq_sum[None, :], axis=1) / members

time: 505 us -> 506 us (level)
    psum x1 -> x0, blocking collectives: 64.2 us -> none  [body(): seq_sum = lax.psum(placed, ('req', 'vocab'))]
    unnamed x1 -> x2, blocking collectives: 127 us -> 192 us
where the time goes in v1:
time: 506 us; the launch traced here: 505 us
  blocking collectives  316 us (62%)
  waiting for transfers between devices  101 us (20%)
  matrix products  47.7 us (9%)
  other arithmetic  17.3 us (3%)
  between operations  15.2 us (3%)
  local copies, waits for them, and re-layouts  8.63 us (2%)
    unnamed x2, blocking collectives  192 us
    pmax x1, blocking collectives, body(): row_top = lax.pmax(maxima, 'vocab')  124 us
    psum x1, waiting for transfers between devices, body(): lax.psum((sums * rescale, moments * rescale, picked), 'vocab')  101 us
    dot_general x12, matrix products, slice_stats(): logits = jnp.dot(block_rows, weight, preferred_element_type=jnp.float32)  47.7 us
    reduce_sum x6, other arithmetic, slice_stats(): moment = jnp.sum(exps * logits, axis=1)  10.3 us
  transfers between devices with their start and end apart: 2, of which 1 were waited for; matrix products, arithmetic and copies ran while one was open for 0% of the time, Pallas kernels for 0%

profile of v1, /device:TPU:1, one launch (start us, length us, event | category | flops | bytes accessed | tf_op | source)
XLA Modules:
  0.0 505.5 jit_solution(15452840009662678816)
XLA Ops:
  7.2 0.0 copy-start.15
  7.2 0.0 copy-start.11
  7.2 0.0 all-gather.3.cloned.1.call-start
  7.2 1.4 fusion.36
  8.6 2.3 fusion.38
  10.9 0.0 all-gather.3.cloned.1.call-update
  11.0 0.0 all-reduce.5.cloned.1.call-start
  11.1 0.0 copy-done.11
  11.1 0.1 reshape.74
  11.2 0.0 copy-done.15
  11.2 0.6 dynamic-slice
  12.4 0.3 dynamic-update-slice
  12.7 127.5 %all-reduce = s32[6144]{0:T(1024)S(1)} all-reduce(s32[6144]{0:T(1024)S(1)} %dynamic-update-slice), channel_id=1, replica_groups=mesh['req'=4,'vocab'=32] {'vocab'}, use_global_device_ids=true, to_apply=%add | all-reduce | flops 6144 | bytes 49152
  140.2 0.0 all-gather.3.cloned.1.call-done
  140.2 0.0 copy-start.12
  140.2 6.6 %fusion.45 = (f32[512]{0:T(512)S(1)}, f32[512,1000]{0,1:T(8,128)}) fusion(bf16[2048,1000]{0,1:T(8,128)(2,1)} %param.8, bf16[6144,2048]{1,0:T(8,128)(2,1)} %all-gather.3.cloned.1.call-done), kind=kOutput, calls=%fused_computation.170 | convolution fusion | flops 2097663488 | bytes 8243200 | tf_op jit(solution)/shard_map/dot_general | solution.py:22
  146.9 4.1 copy-done.12
  150.9 5.9 %fusion.46 = (f32[512]{0:T(512)S(1)}, f32[512,1000]{0,1:T(8,128)}) fusion(bf16[2048,1000]{0,1:T(8,128)(2,1)} %param.8, bf16[6144,2048]{1,0:T(8,128)(2,1)S(1)} %copy-done.12), kind=kOutput, calls=%fused_computation.171 | convolution fusion | flops 2097663488 | bytes 8243200 | tf_op jit(solution)/shard_map/dot_general | solution.py:22
  156.9 0.0 copy-done.13
  156.9 3.6 fusion.47
  160.5 3.6 fusion.48
  164.1 3.7 fusion.49
  167.8 3.6 fusion.50
  171.5 3.8 fusion.51
  175.3 3.6 fusion.52
  178.9 3.6 fusion.53
  182.6 3.6 fusion.54
  186.2 2.3 fusion.55
  188.5 3.6 fusion.56
  192.1 124.0 %pmax.7 = f32[6144]{0:T(1024)S(1)} all-reduce(f32[6144]{0:T(1024)S(1)} %constant_dynamic-update-slice_fusion.1), channel_id=1, replica_groups=mesh['req'=4,'vocab'=32] {'vocab'}, use_global_device_ids=true, to_apply=%region_26.27 | all-reduce | flops 6144 | bytes 49152 | tf_op jit(solution)/shard_map/pmax | solution.py:52
  316.1 3.7 multiply_reduce_fusion.10
  319.8 0.0 copy-done.7
  319.8 0.0 copy-done.8
  319.8 0.0 copy-start.5
  319.8 0.0 copy-start.6
  319.8 1.3 multiply_reduce_fusion.8
  321.2 0.2 copy-done.5
  321.4 0.6 copy-done.6
  322.0 1.3 multiply_reduce_fusion.6
  323.4 0.2 copy-done.3
  323.6 0.6 copy-done.4
  324.2 1.3 multiply_reduce_fusion.4
  325.6 0.2 copy-done.1
  325.8 0.6 copy-done.2
  326.4 1.3 multiply_reduce_fusion.2
  327.8 0.2 copy-done
  328.0 1.3 multiply_reduce_fusion
  329.6 0.6 fusion.39
  330.3 0.0 copy-done.9
  330.3 0.0 all-reduce.5.cloned.1.call-update
  330.3 0.0 copy-done.14
  330.3 0.1 dynamic_slice.15
  330.4 100.8 %all-reduce.5.cloned.1.call-done = (f32[6144]{0:T(1024)}, f32[6144]{0:T(1024)}, f32[6144]{0:T(1024)}) async-done(((f32[6144]{0:T(1024)}, f32[6144]{0:T(1024)}, f32[6144]{0:T(1024)}), (f32[6144]{0:T(1024)}, f32[6144]{0:T(1024)}, f32[6144]{0:T(1024)})) %all-reduce.5.cloned.1.call-update) | async-done | bytes 73744 | tf_op jit(solution)/shard_map/psum | solution.py:54
  431.3 0.8 divide_subtract_fusion
  432.1 0.1 reshape.71
  432.2 0.1 reshape.72
  432.2 0.8 fusion.44
  433.0 0.1 select_reduce_fusion.12
  433.1 0.3 dynamic-update-slice.1
  433.4 64.2 %all-reduce.1 = f32[2048]{0:T(1024)S(1)} all-reduce(f32[2048]{0:T(1024)S(1)} %dynamic-update-slice.1), channel_id=2, replica_groups=mesh['req'=4,'vocab'=32] {'req','vocab'}, use_global_device_ids=true, to_apply=%add.1 | all-reduce | flops 2048 | bytes 16384
  497.6 0.1 reshape.73
  497.7 0.2 fusion.42
  497.9 0.2 fusion.43
  498.1 0.5 maximum_divide_fusion
  (72 shorter events, 0.4 us)
Async XLA Ops:
  7.2 4.0 copy-start.15
  7.2 3.9 copy-start.11
  7.2 133.0 %all-gather.3.cloned.1.call-start = ((), (), s32[]{:S(2)}) async-start(), calls=%async_computation | async-start | bytes 25952256 | tf_op jit(solution)/shard_map/all_gather | solution.py:45
  11.0 420.3 %all-reduce.5.cloned.1.call-start = ((), (), s32[]{:S(2)}) async-start(), calls=%async_computation.1 | async-start | bytes 147456 | tf_op jit(solution)/shard_map/psum | solution.py:54
  140.2 10.7 %copy-start.12 = (bf16[6144,2048]{1,0:T(8,128)(2,1)S(1)}, bf16[6144,2048]{1,0:T(8,128)(2,1)}, u32[]{:S(2)}) copy-start(bf16[6144,2048]{1,0:T(8,128)(2,1)} %all-gather.3.cloned.1.call-done) | copy-start | bytes 75497472
  150.9 5.9 %copy-start.13 = (bf16[2048,1000]{0,1:T(8,128)(2,1)S(1)}, bf16[2048,1000]{0,1:T(8,128)(2,1)}, u32[]{:S(2)}) copy-start(bf16[2048,1000]{0,1:T(8,128)(2,1)} %param.8) | copy-start | bytes 12288004
  316.1 3.7 copy-start.7
  316.1 3.7 copy-start.8
  319.8 1.6 copy-start.5
  319.8 2.2 copy-start.6
  322.0 1.6 copy-start.3
  322.0 2.2 copy-start.4
  324.2 1.6 copy-start.1
  324.2 2.2 copy-start.2
  326.4 1.6 copy-start
  328.0 2.4 copy-start.14
  328.0 169.7 %copy-start.10 = (s32[16]{0:T(128)S(1)}, s32[16]{0:T(128)}, u32[]{:S(2)}) copy-start(s32[16]{0:T(128)} %param.11) | copy-start | bytes 196
  329.6 0.6 copy-start.9
Sparse Core Ops, SparseCore 0:
  11.1 95.8 all-gather.2
  330.4 100.7 all-reduce.4
